TPU v7x, 32 devices: a whole 2x2x4 slice. The times are simulated.
32 devices in a mesh: gx: 8 (over z, y), gy: 4 (over x, core).
Axes of the slice: x: 2, y: 2, z: 4, core: 2. Of those that a mesh axis runs over, the one named last changes fastest.
Arguments:
- volume: bfloat16 [256, 128, 2048], P('gx', 'gy'), may hold values from -60 to 60, as said below
- tissue: int32 [16, 8, 2], P(None, 'gy'), may hold values from 0 to 1, as said below
- w_conv: bfloat16 [3, 3, 3, 64, 128], replicated, may hold values from -0.15625 to 0.15625
- gamma: float32 [128], replicated, may hold values from 0.5 to 1.5
- beta: float32 [128], replicated, may hold values from -3 to 3
- w_down: bfloat16 [2, 2, 2, 128, 128], replicated, may hold values from -0.1875 to 0.1875
- b_down: float32 [128], replicated, may hold values from -3 to 3
Outputs:
- features: bfloat16 [128, 64, 2048], P('gx', 'gy')
Inputs may be any that keep to these rules, and one draw needn't show every extreme that they name: In every draw some device's 4 * 2 tiles all have tissue = 1; the tiles with tissue differ in number from device to device. `volume`: voxel and channel scales vary.
All inputs are finite; a program needn't handle non-finite values.
Results may differ from a plain program's by a relative error of at most 0.0046.
Values may be sent and summed in bfloat16 or wider, within the bound.
No kernel may reach another device: no remote copies, remote signals or barrier semaphores. Data moves between devices by JAX's collectives and lax.ppermute only.
A program may use at most 128 MiB of HBM per device.

v0:
```python
import jax
import jax.numpy as jnp
from jax import lax
from jax.sharding import PartitionSpec as P

CIN = 64
CMID = 128
COUT = 128
GROUPS = 8
TILE = 16


def with_halo(block, sides, width):
    for axis, dim in sides:
        count = lax.axis_size(axis)
        forward = [(i, i + 1) for i in range(count - 1)]
        backward = [(target, source) for source, target in forward]
        low = lax.ppermute(
            lax.slice_in_dim(block, block.shape[dim] - width, None, axis=dim), axis, forward
        )
        high = lax.ppermute(lax.slice_in_dim(block, 0, width, axis=dim), axis, backward)
        block = jnp.concatenate([low, block, high], axis=dim)
    return block


def build_band(w_conv):
    in_pos = jnp.arange(6, dtype=jnp.int32)[:, None, None]
    out_pos = jnp.arange(4, dtype=jnp.int32)[None, :, None]
    taps = jnp.arange(3, dtype=jnp.int32)[None, None, :]
    select = (in_pos - out_pos == taps).astype(jnp.float32)
    band = jnp.einsum("zod,xydcm->xyzcom", select, w_conv.astype(jnp.float32))
    return band.reshape(3, 3, 6 * CIN, 4 * CMID).astype(jnp.bfloat16)


def tile_features(window, band, gamma, beta, w_down, b_down):
    side_cells = window.shape[0] - 2
    z_blocks = side_cells // 4
    outputs = []
    for block_index in range(z_blocks):
        summed = jnp.zeros((side_cells * side_cells, 4 * CMID), jnp.float32)
        for tap_index in range(9):
            shift_x = tap_index // 3
            shift_y = tap_index % 3
            slab = window[
                shift_x : shift_x + side_cells,
                shift_y : shift_y + side_cells,
                4 * block_index * CIN : (4 * block_index + 6) * CIN,
            ]
            slab = slab.reshape(side_cells * side_cells, 6 * CIN)
            summed = summed + jnp.dot(
                slab, band[shift_x, shift_y], preferred_element_type=jnp.float32
            )
        outputs.append(summed)
    summed = jnp.concatenate(outputs, axis=1)
    grouped = summed.reshape(side_cells * side_cells, side_cells, GROUPS, CMID // GROUPS)
    group_mean = jnp.mean(grouped, axis=(0, 1, 3), keepdims=True)
    group_var = jnp.mean(jnp.square(grouped - group_mean), axis=(0, 1, 3), keepdims=True)
    normed = ((grouped - group_mean) * lax.rsqrt(group_var + 1e-05)).reshape(
        side_cells * side_cells, side_cells * CMID
    )
    active = jnp.maximum(
        normed * jnp.tile(gamma, side_cells) + jnp.tile(beta, side_cells), 0.0
    ).astype(jnp.bfloat16)
    half_side = side_cells // 2
    blocks = active.reshape(half_side, 2, half_side, 2, side_cells * CMID)
    pooled = jnp.zeros((half_side**3, COUT), jnp.float32) + b_down
    for corner_index in range(4):
        pick_a = corner_index // 2
        pick_b = corner_index % 2
        corner = blocks[:, pick_a, :, pick_b, :].reshape(half_side**3, 2 * CMID)
        weight_pair = w_down[pick_a, pick_b].reshape(2 * CMID, COUT)
        pooled = pooled + jnp.dot(corner, weight_pair, preferred_element_type=jnp.float32)
    return pooled.astype(jnp.bfloat16).reshape(half_side, half_side, half_side * COUT)


def compact_order(valid_flags):
    length = valid_flags.shape[0]
    indices = jnp.arange(length, dtype=jnp.int32)
    flag_ranks = jnp.cumsum(valid_flags) - 1
    matches = (valid_flags[:, None] > 0) & (flag_ranks[:, None] == indices[None, :])
    return (
        jnp.sum(jnp.where(matches, indices[:, None], 0), axis=0),
        flag_ranks,
        jnp.sum(valid_flags),
    )


def shards(volume, tissue, w_conv, gamma, beta, w_down, b_down):
    peer_count = lax.axis_size("gx")
    own_index = lax.axis_index("gx")
    grown = with_halo(volume, (("gx", 0), ("gy", 1)), 1)
    band = build_band(w_conv)
    depth_cells = volume.shape[2] // CIN
    padded = jnp.pad(grown, ((0, 0), (0, 0), (CIN, CIN)))
    layers = depth_cells // TILE
    local_tiles = 4 * layers
    half_side = TILE // 2
    tile_shape = (half_side, half_side, half_side * COUT)
    own_tissue = lax.dynamic_slice_in_dim(tissue, own_index * 2, 2, 0).reshape(local_tiles)
    tile_of_rank, tile_ranks, occupied = compact_order(own_tissue)
    slot_count = -(-local_tiles // peer_count)
    slot_total = peer_count * slot_count
    targets = jnp.arange(peer_count, dtype=jnp.int32)[:, None]
    slot_ids = jnp.arange(slot_count, dtype=jnp.int32)[None, :]
    tile_loads = jnp.sum(tissue.reshape(peer_count, local_tiles), axis=1)

    def window_at(tile_id):
        pos_a = tile_id // (2 * layers)
        pos_b = tile_id // layers % 2
        pos_c = tile_id % layers
        return lax.dynamic_slice(
            padded,
            (pos_a * TILE, pos_b * TILE, pos_c * TILE * CIN),
            (TILE + 2, TILE + 2, (TILE + 2) * CIN),
        )

    def features_of(window):
        return tile_features(window, band, gamma, beta, w_down, b_down)

    offsets = (jnp.cumsum(tile_loads) - tile_loads) % peer_count
    own_offset = offsets[own_index]
    wanted = slot_ids * peer_count + (targets - own_offset) % peer_count
    sending = (wanted < occupied).reshape(-1)
    picks = tile_of_rank[jnp.minimum(wanted, local_tiles - 1).reshape(-1)]
    windows = jax.vmap(window_at)(picks)
    windows = jnp.where(sending[:, None, None, None], windows, jnp.zeros((), jnp.bfloat16))
    incoming = lax.all_to_all(
        windows.reshape(peer_count, slot_count, TILE + 2, TILE + 2, (TILE + 2) * CIN),
        "gx",
        split_axis=0,
        concat_axis=0,
        tiled=True,
    )
    arrived = (
        slot_ids * peer_count + (own_index - offsets[:, None]) % peer_count < tile_loads[:, None]
    )
    slot_of_rank, unused_ranks, received = compact_order(arrived.reshape(-1).astype(jnp.int32))
    arrived_stack = incoming.reshape(slot_total, TILE + 2, TILE + 2, (TILE + 2) * CIN)

    def compute(rank_id, buffer):
        slot_id = slot_of_rank[rank_id]
        return lax.dynamic_update_index_in_dim(
            buffer, features_of(arrived_stack[slot_id]), slot_id, 0
        )

    results = lax.fori_loop(
        0, received, compute, jnp.zeros((slot_total,) + tile_shape, jnp.bfloat16)
    )
    replies = lax.all_to_all(
        results.reshape(peer_count, slot_count, half_side, half_side, half_side * COUT),
        "gx",
        split_axis=0,
        concat_axis=0,
        tiled=True,
    )
    own_offset = offsets[own_index]
    answers = replies.reshape(slot_total, half_side, half_side, half_side * COUT)
    where_from = (own_offset + tile_ranks) % peer_count * slot_count + tile_ranks // peer_count
    picked = answers[jnp.clip(where_from, 0, slot_total - 1)]
    tile_stack = jnp.where(own_tissue[:, None, None, None] > 0, picked, jnp.zeros((), jnp.bfloat16))
    tile_stack = tile_stack.reshape(2, 2, layers, half_side, half_side, half_side * COUT)
    tile_stack = tile_stack.transpose(0, 3, 1, 4, 2, 5)
    return tile_stack.reshape(TILE, TILE, layers * half_side * COUT)


def solution(mesh):
    in_specs = (P("gx", "gy", None), P(None, "gy", None), P(), P(), P(), P(), P())
    out_specs = P("gx", "gy", None)
    return jax.shard_map(shards, mesh=mesh, in_specs=in_specs, out_specs=out_specs, check_vma=False)
```

profile of v0, /device:TPU:2, one launch (start us, length us, event | category | flops | bytes accessed | tf_op | source)
XLA Modules:
  0.0 685.5 jit_solution(18252681644420043497)
XLA Ops:
  1.0 3.4 collective-permute-start
  11.5 2.5 constant_dynamic-update-slice_fusion.2
  18.5 3.6 collective-permute-start.3
  26.2 10.8 %fusion.88 = bf16[34,34,2176]{2,1,0:T(8,128)(2,1)} fusion(bf16[34,1,2048]{2,1,0:T(2,128)(2,1)S(1)} %collective-permute-done.3, bf16[34,32,2048]{2,1,0:T(8,128)(2,1)} %copy-done.3, bf16[34,1,2048]{2,1,0:T(2,128)(2,1)S(1)} %collective-permute-done.2), kind=kLoop, calls=%fused_computation.140 | loop fusion | flops 30185472 | bytes 9765888 | tf_op jit(solution)/shard_map/concatenate | solution.py:22
  37.0 44.0 %while.12 = (s32[]{:T(128)}, bf16[34,34,2176]{2,1,0:T(8,128)(2,1)}, s32[8,3]{0,1:T(4,128)S(1)}, bf16[8,18,18,1152]{3,2,1,0:T(8,128)(2,1)}, s32[]{:T(128)}) while((s32[]{:T(128)}, bf16[34,34,2176]{2,1,0:T(8,128)(2,1)}, s32[8,3]{0,1:T(4,128)S(1)}, bf16[8,18,18,1152]{3,2,1,0:T(8,128)(2,1)}, s32[]{:T(128)}) %tuple.93), condition=%wide.while_cond, body=%wide.while_body.sunk | while | flops 2 | bytes 1992817 | solution.py:111
  37.7 4.8 bitcast_dynamic-update-slice_fusion.2
  43.1 4.8 bitcast_dynamic-update-slice_fusion.2
  48.5 4.8 bitcast_dynamic-update-slice_fusion.2
  54.0 4.9 bitcast_dynamic-update-slice_fusion.2
  59.5 4.9 bitcast_dynamic-update-slice_fusion.2
  65.0 4.9 bitcast_dynamic-update-slice_fusion.2
  70.6 4.9 bitcast_dynamic-update-slice_fusion.2
  76.1 4.9 bitcast_dynamic-update-slice_fusion.2
  81.0 7.2 %bitcast_select_fusion = bf16[8,1,18,18,1152]{4,3,2,1,0:T(8,128)(2,1)} fusion(bf16[8,18,18,1152]{3,2,1,0:T(8,128)(2,1)} %get-tuple-element.66, pred[8]{0:T(512)(128)(4,1)S(1)} %fusion.98), kind=kLoop, calls=%fused_computation.135 | loop fusion | flops 2985984 | bytes 11943944 | tf_op jit(solution)/shard_map/jit(_where)/select_n | solution.py:126
  88.2 7.3 %all-to-all-start = ((bf16[8,1,18,18,1152]{4,3,2,1,0:T(8,128)(2,1)}), bf16[8,1,18,18,1152]{4,3,2,1,0:T(8,128)(2,1)}, u32[]{:S(2)}, u32[]{:S(2)}) async-start(bf16[8,1,18,18,1152]{4,3,2,1,0:T(8,128)(2,1)} %bitcast_select_fusion), calls=%async_computation | async-start | bytes 15925248 | tf_op jit(solution)/shard_map/all_to_all | solution.py:127
  98.5 4.5 copy.41
  103.0 5.6 convert_element_type.39
  108.7 157.0 %all-to-all-done = bf16[8,1,18,18,1152]{4,3,2,1,0:T(8,128)(2,1)} async-done(((bf16[8,1,18,18,1152]{4,3,2,1,0:T(8,128)(2,1)}), bf16[8,1,18,18,1152]{4,3,2,1,0:T(8,128)(2,1)}, u32[]{:S(2)}, u32[]{:S(2)}) %all-to-all-start) | async-done | bytes 5972000 | tf_op jit(solution)/shard_map/all_to_all | solution.py:127
  266.9 396.9 %while.11 = (s32[]{:T(128)}, bf16[8,8,8,1024]{3,2,1,0:T(8,128)(2,1)}, s32[]{:T(128)}, f32[128]{0:T(128)}, s32[8]{0:T(128)S(1)}, /*index=5*/bf16[8,18,18,1152]{3,...) while((s32[]{:T(128)}, ...), condition=%wide.region_14.15_spmd, body=%wide.region_9.14_spmd.sunk | while | flops 3772579840 | bytes 102986096 | solution.py:146
  294.1 2.1 concatenate.34
  360.2 2.1 concatenate.34
  426.2 2.1 concatenate.34
  663.8 3.6 all-to-all-start.1
  668.0 15.6 %all-to-all-done.1 = bf16[8,1,8,8,1024]{4,3,2,1,0:T(8,128)(2,1)S(1)} async-done(((bf16[8,1,8,8,1024]{4,3,2,1,0:T(8,128)(2,1)}), bf16[8,1,8,8,1024]{4,3,2,1,0:T(8,128)(2,1)S(1)}, u32[]{:S(2)}, u32[]{:S(2)}) %all-to-all-start.1) | async-done | bytes 1048608 | tf_op jit(solution)/shard_map/all_to_all | solution.py:149
  (568 shorter events, 399.2 us)
Async XLA Ops:
  1.0 10.5 %collective-permute-start = (bf16[1,32,2048]{2,1,0:T(8,128)(2,1)S(1)}, bf16[1,32,2048]{2,1,0:T(8,128)(2,1)S(1)}, u32[]{:S(2)}, u32[]{:S(2)}) collective-permute-start(bf16[1,32,2048]{2,1,0:T(8,128)(2,1)S(1)} %get-tuple-element.152), channel_id=1, source_target_pairs={{0,4},{4,8},{8,12},{12,16},{16,20},{20,24},{24,28},{1,5},{5,9},{9,... | collective-permute-start | bytes 393224 | tf_op jit(solution)/shard_map/ppermute | solution.py:18
  4.4 9.6 %collective-permute-start.1 = (bf16[1,32,2048]{2,1,0:T(8,128)(2,1)S(1)}, bf16[1,32,2048]{2,1,0:T(8,128)(2,1)S(1)}, u32[]{:S(2)}, u32[]{:S(2)}) collective-permute-start(bf16[1,32,2048]{2,1,0:T(8,128)(2,1)S(1)} %get-tuple-element.151), channel_id=1, source_target_pairs={{4,0},{8,4},{12,8},{16,12},{20,16},{24,20},{28,24},{5,1},{9,5},{13... | collective-permute-start | bytes 393224 | tf_op jit(solution)/shard_map/ppermute | solution.py:21
  16.5 7.9 %collective-permute-start.2 = (bf16[34,1,2048]{2,1,0:T(2,128)(2,1)S(1)}, bf16[34,1,2048]{2,1,0:T(2,128)(2,1)S(1)}, u32[]{:S(2)}, u32[]{:S(2)}) collective-permute-start(bf16[34,1,2048]{2,1,0:T(2,128)(2,1)S(1)} %get-tuple-element.149), channel_id=1, source_target_pairs={{0,1},{1,2},{2,3},{4,5},{5,6},{6,7},{8,9},{9,10},{10,11},{12,13},{... | collective-permute-start | bytes 417800 | tf_op jit(solution)/shard_map/ppermute | solution.py:18
  18.5 7.7 %collective-permute-start.3 = (bf16[34,1,2048]{2,1,0:T(2,128)(2,1)S(1)}, bf16[34,1,2048]{2,1,0:T(2,128)(2,1)S(1)}, u32[]{:S(2)}, u32[]{:S(2)}) collective-permute-start(bf16[34,1,2048]{2,1,0:T(2,128)(2,1)S(1)} %get-tuple-element.150), channel_id=1, source_target_pairs={{1,0},{2,1},{3,2},{5,4},{6,5},{7,6},{9,8},{10,9},{11,10},{13,12},{... | collective-permute-start | bytes 417800 | tf_op jit(solution)/shard_map/ppermute | solution.py:21
  88.2 8.2 %copy-start.4 = (bf16[3,3,3,64,128]{4,3,2,1,0:T(8,128)(2,1)S(1)}, bf16[3,3,3,64,128]{4,3,2,1,0:T(8,128)(2,1)}, u32[]{:S(2)}) copy-start(bf16[3,3,3,64,128]{4,3,2,1,0:T(8,128)(2,1)} %param.11) | copy-start | bytes 1327108
  88.2 177.6 %all-to-all-start = ((bf16[8,1,18,18,1152]{4,3,2,1,0:T(8,128)(2,1)}), bf16[8,1,18,18,1152]{4,3,2,1,0:T(8,128)(2,1)}, u32[]{:S(2)}, u32[]{:S(2)}) async-start(bf16[8,1,18,18,1152]{4,3,2,1,0:T(8,128)(2,1)} %bitcast_select_fusion), calls=%async_computation | async-start | bytes 15925248 | tf_op jit(solution)/shard_map/all_to_all | solution.py:127
  275.4 9.2 %copy-start = (f32[256,512]{1,0:T(8,128)}, f32[256,512]{1,0:T(8,128)S(1)}, u32[]{:S(2)}) copy-start(f32[256,512]{1,0:T(8,128)S(1)} %convolution_add_fusion.102) | copy-start | bytes 1572868 | tf_op jit(solution)/shard_map/while
  278.2 6.4 copy-start.1
  313.2 19.9 %copy-start.8 = (s32[8]{0:T(128)S(1)}, s32[8]{0:T(128)}, u32[]{:S(2)}) copy-start(s32[8]{0:T(128)} %copy-done.7) | copy-start | bytes 100 | tf_op jit(solution)/shard_map/while
  341.4 9.2 %copy-start = (f32[256,512]{1,0:T(8,128)}, f32[256,512]{1,0:T(8,128)S(1)}, u32[]{:S(2)}) copy-start(f32[256,512]{1,0:T(8,128)S(1)} %convolution_add_fusion.102) | copy-start | bytes 1572868 | tf_op jit(solution)/shard_map/while
  344.2 6.4 copy-start.1
  379.2 19.9 %copy-start.8 = (s32[8]{0:T(128)S(1)}, s32[8]{0:T(128)}, u32[]{:S(2)}) copy-start(s32[8]{0:T(128)} %copy-done.7) | copy-start | bytes 100 | tf_op jit(solution)/shard_map/while
  407.4 9.2 %copy-start = (f32[256,512]{1,0:T(8,128)}, f32[256,512]{1,0:T(8,128)S(1)}, u32[]{:S(2)}) copy-start(f32[256,512]{1,0:T(8,128)S(1)} %convolution_add_fusion.102) | copy-start | bytes 1572868 | tf_op jit(solution)/shard_map/while
  410.2 6.4 copy-start.1
  445.2 19.9 %copy-start.8 = (s32[8]{0:T(128)S(1)}, s32[8]{0:T(128)}, u32[]{:S(2)}) copy-start(s32[8]{0:T(128)} %copy-done.7) | copy-start | bytes 100 | tf_op jit(solution)/shard_map/while
  473.4 9.2 %copy-start = (f32[256,512]{1,0:T(8,128)}, f32[256,512]{1,0:T(8,128)S(1)}, u32[]{:S(2)}) copy-start(f32[256,512]{1,0:T(8,128)S(1)} %convolution_add_fusion.102) | copy-start | bytes 1572868 | tf_op jit(solution)/shard_map/while
  476.2 6.4 copy-start.1
  511.2 19.9 %copy-start.8 = (s32[8]{0:T(128)S(1)}, s32[8]{0:T(128)}, u32[]{:S(2)}) copy-start(s32[8]{0:T(128)} %copy-done.7) | copy-start | bytes 100 | tf_op jit(solution)/shard_map/while
  539.4 9.2 %copy-start = (f32[256,512]{1,0:T(8,128)}, f32[256,512]{1,0:T(8,128)S(1)}, u32[]{:S(2)}) copy-start(f32[256,512]{1,0:T(8,128)S(1)} %convolution_add_fusion.102) | copy-start | bytes 1572868 | tf_op jit(solution)/shard_map/while
  577.2 19.9 %copy-start.8 = (s32[8]{0:T(128)S(1)}, s32[8]{0:T(128)}, u32[]{:S(2)}) copy-start(s32[8]{0:T(128)} %copy-done.7) | copy-start | bytes 100 | tf_op jit(solution)/shard_map/while
  605.4 9.2 %copy-start = (f32[256,512]{1,0:T(8,128)}, f32[256,512]{1,0:T(8,128)S(1)}, u32[]{:S(2)}) copy-start(f32[256,512]{1,0:T(8,128)S(1)} %convolution_add_fusion.102) | copy-start | bytes 1572868 | tf_op jit(solution)/shard_map/while
  643.2 19.9 %copy-start.8 = (s32[8]{0:T(128)S(1)}, s32[8]{0:T(128)}, u32[]{:S(2)}) copy-start(s32[8]{0:T(128)} %copy-done.7) | copy-start | bytes 100 | tf_op jit(solution)/shard_map/while
  663.8 20.5 %copy-start.6 = (pred[2,2,2]{2,1,0:T(4,128)(4,1)S(1)}, pred[2,2,2]{2,1,0:T(4,128)(4,1)}, u32[]{:S(2)}) copy-start(pred[2,2,2]{2,1,0:T(4,128)(4,1)} %copy-done.5) | copy-start | bytes 28
  663.8 19.9 %all-to-all-start.1 = ((bf16[8,1,8,8,1024]{4,3,2,1,0:T(8,128)(2,1)}), bf16[8,1,8,8,1024]{4,3,2,1,0:T(8,128)(2,1)S(1)}, u32[]{:S(2)}, u32[]{:S(2)}) async-start(bf16[8,1,8,8,1024]{4,3,2,1,0:T(8,128)(2,1)} %bitcast.543), calls=%async_computation.1 | async-start | bytes 2097152 | tf_op jit(solution)/shard_map/all_to_all | solution.py:149
  (16 other events, 65.3 us)
where the time goes:
time: 693 us; the launch traced here: 686 us
  local copies, waits for them, and re-layouts  285 us (41%)
  waiting for transfers between devices  175 us (25%)
  matrix products  119 us (17%)
  other arithmetic  64.9 us (9%)
  starting transfers between devices  21.1 us (3%)
  loops' own time  19.7 us (3%)
    all_to_all x1, waiting for transfers between devices, shards(): lax.all_to_all(windows.reshape(peer_count, slot_count, TILE + 2, TILE + 2...  157 us
    concatenate x48, local copies, waits for them, and re-layouts, tile_features(): summed = jnp.concatenate(outputs, axis=1)  93.1 us
    dot_general x216, matrix products, tile_features(): jnp.dot(slab, band[shift_x, shift_y], preferred_element_type=jnp.float32)  70 us
    dot_general x24, matrix products, tile_features(): jnp.dot(corner, weight_pair, preferred_element_type=jnp.float32)  47.3 us
    gather x24, local copies, waits for them, and re-layouts  44 us
    squeeze x24, local copies, waits for them, and re-layouts, tile_features(): corner = blocks[:, pick_a, :, pick_b, :].reshape(half_side ** 3, 2 * CMID)  43.1 us
    another operation x1, loops' own time, shards(): lax.fori_loop(0, received, compute, jnp.zeros((slot_total,) + tile_shape,...  19.7 us
    reduce_sum x12, other arithmetic, tile_features(): jnp.mean(jnp.square(grouped - group_mean), axis=(0, 1, 3), keepdims=True)  16.4 us
  transfers between devices with their start and end apart: 6, of which 4 were waited for; matrix products, arithmetic and copies ran while one was open for 3% of the time, Pallas kernels for 0%

commit v1 on v0

v1 whole, which is shorter than its diff:
```python
import jax
import jax.numpy as jnp
from jax import lax
from jax.experimental import pallas as pl
from jax.experimental.pallas import tpu as pltpu
from jax.sharding import PartitionSpec as P

CIN = 64
CMID = 128
COUT = 128
GROUPS = 8
TILE = 16
EPS = 1e-05


def with_halo(block, sides, width):
    for axis, dim in sides:
        count = lax.axis_size(axis)
        forward = [(i, i + 1) for i in range(count - 1)]
        backward = [(target, source) for source, target in forward]
        low = lax.ppermute(
            lax.slice_in_dim(block, block.shape[dim] - width, None, axis=dim), axis, forward
        )
        high = lax.ppermute(lax.slice_in_dim(block, 0, width, axis=dim), axis, backward)
        block = jnp.concatenate([low, block, high], axis=dim)
    return block


def build_band(w_conv):
    in_pos = jnp.arange(4, dtype=jnp.int32)[:, None, None]
    out_pos = jnp.arange(2, dtype=jnp.int32)[None, :, None]
    taps = jnp.arange(3, dtype=jnp.int32)[None, None, :]
    select = (in_pos - out_pos == taps).astype(jnp.float32)
    band = jnp.einsum("zod,xydcm->xyzcom", select, w_conv.astype(jnp.float32))
    return band.reshape(9, 4 * CIN, 2 * CMID).astype(jnp.bfloat16)


def group_sum(row, indicator):
    row = jnp.broadcast_to(row, (8, row.shape[1]))
    total = jnp.zeros(row.shape, jnp.float32)
    rest = row
    for _ in range(3):
        piece = rest.astype(jnp.bfloat16)
        total = total + jnp.dot(piece, indicator, preferred_element_type=jnp.float32)
        rest = rest - piece.astype(jnp.float32)
    return total[0:1]


def tile_kernel(flags_ref, win_ref, band_ref, ind_ref, gamma_ref, beta_ref, down_ref,
                bias_ref, out_ref, conv_ref):
    tile = pl.program_id(0)
    rows = TILE * TILE
    pairs = TILE // 2
    half = TILE // 2

    @pl.when(flags_ref[tile] > 0)
    def _():
        for pair in range(pairs):
            acc = None
            for tap in range(9):
                shift_x, shift_y = tap // 3, tap % 3
                slab = win_ref[0, shift_y, shift_x:shift_x + TILE, :,
                               2 * CIN * pair:2 * CIN * pair + 4 * CIN]
                part = jnp.dot(slab.reshape(rows, 4 * CIN), band_ref[tap],
                               preferred_element_type=jnp.float32)
                acc = part if acc is None else acc + part
            conv_ref[2 * pair] = acc[:, :CMID]
            conv_ref[2 * pair + 1] = acc[:, CMID:]

        count = float(rows * TILE * (CMID // GROUPS))
        indicator = ind_ref[...]
        total = jnp.zeros((1, CMID), jnp.float32)
        for depth in range(TILE):
            total = total + jnp.sum(conv_ref[depth], axis=0, keepdims=True)
        mean = group_sum(total, indicator) / count
        total = jnp.zeros((1, CMID), jnp.float32)
        for depth in range(TILE):
            diff = conv_ref[depth] - mean
            total = total + jnp.sum(diff * diff, axis=0, keepdims=True)
        var = group_sum(total, indicator) / count
        scale = lax.rsqrt(var + EPS) * gamma_ref[...]
        shift = beta_ref[...]
        for depth in range(TILE):
            conv_ref[depth] = jnp.maximum((conv_ref[depth] - mean) * scale + shift, 0.0)

        results = [jnp.zeros((half * half, COUT), jnp.float32) for _ in range(half)]
        for pick_b in range(2):
            picked = conv_ref[:, pl.ds(pick_b, rows // 2, stride=2), :]
            for pick_a in range(2):
                corners = [
                    picked[depth].reshape(half, 2, half, CMID)[:, pick_a]
                    .reshape(half * half, CMID).astype(jnp.bfloat16)
                    for depth in range(TILE)
                ]
                weight = down_ref[pick_a * 2 + pick_b]
                for depth in range(half):
                    lhs = jnp.concatenate([corners[2 * depth], corners[2 * depth + 1]], axis=1)
                    results[depth] = results[depth] + jnp.dot(
                        lhs, weight, preferred_element_type=jnp.float32)
        bias = bias_ref[...]
        out_ref[0] = jnp.concatenate([r + bias for r in results], axis=1).astype(jnp.bfloat16)

    @pl.when(flags_ref[tile] == 0)
    def _():
        out_ref[...] = jnp.zeros(out_ref.shape, out_ref.dtype)


def shards(volume, tissue, w_conv, gamma, beta, w_down, b_down):
    own_index = lax.axis_index("gx")
    size_x, size_y, merged = volume.shape
    size_z = merged // CIN
    tiles_x, tiles_y, tiles_z = size_x // TILE, size_y // TILE, size_z // TILE
    tile_count = tiles_x * tiles_y * tiles_z
    half = TILE // 2
    grown = with_halo(volume, (("gx", 0), ("gy", 1)), 1)
    grown = jnp.pad(grown, ((0, 0), (0, 0), (CIN, CIN)))
    depth_lanes = (TILE + 2) * CIN
    windows = []
    for i in range(tiles_x):
        for j in range(tiles_y):
            for k in range(tiles_z):
                shifted = [
                    grown[TILE * i:TILE * i + TILE + 2, TILE * j + dy:TILE * j + dy + TILE,
                          TILE * CIN * k:TILE * CIN * k + depth_lanes]
                    for dy in range(3)
                ]
                windows.append(jnp.stack(shifted))
    windows = jnp.stack(windows)
    band = build_band(w_conv)
    lane = jnp.arange(CMID, dtype=jnp.int32)
    group_size = CMID // GROUPS
    indicator = (lane[:, None] // group_size == lane[None, :] // group_size).astype(jnp.bfloat16)
    down = w_down.reshape(4, 2 * CMID, COUT)
    own_tissue = lax.dynamic_slice_in_dim(tissue, own_index * tiles_x, tiles_x, 0)
    flags = own_tissue.reshape(tile_count).astype(jnp.int32)

    full = lambda shape: pl.BlockSpec(shape, lambda t, f: (0,) * len(shape))
    grid_spec = pltpu.PrefetchScalarGridSpec(
        num_scalar_prefetch=1,
        grid=(tile_count,),
        in_specs=[
            pl.BlockSpec((1, 3, TILE + 2, TILE, depth_lanes), lambda t, f: (t, 0, 0, 0, 0)),
            full((9, 4 * CIN, 2 * CMID)),
            full((CMID, CMID)),
            full((1, CMID)),
            full((1, CMID)),
            full((4, 2 * CMID, COUT)),
            full((1, COUT)),
        ],
        out_specs=pl.BlockSpec((1, half * half, half * COUT), lambda t, f: (t, 0, 0)),
        scratch_shapes=[pltpu.VMEM((TILE, TILE * TILE, CMID), jnp.float32)],
    )
    result = pl.pallas_call(
        tile_kernel,
        grid_spec=grid_spec,
        out_shape=jax.ShapeDtypeStruct((tile_count, half * half, half * COUT), jnp.bfloat16),
    )(
        flags,
        windows,
        band,
        indicator,
        gamma.reshape(1, CMID),
        beta.reshape(1, CMID),
        down,
        b_down.reshape(1, COUT),
    )
    result = result.reshape(tiles_x, tiles_y, tiles_z, half, half, half * COUT)
    result = result.transpose(0, 3, 1, 4, 2, 5)
    return result.reshape(size_x // 2, size_y // 2, size_z // 2 * COUT)


def solution(mesh):
    in_specs = (P("gx", "gy", None), P(None, "gy", None), P(), P(), P(), P(), P())
    out_specs = P("gx", "gy", None)
    return jax.shard_map(shards, mesh=mesh, in_specs=in_specs, out_specs=out_specs, check_vma=False)
```

time: 693 us -> 92.1 us (0.13)
  the two profiles are of different devices: /device:TPU:2 before, /device:TPU:21 now
where the time goes in v1:
time: 92.1 us; the launch traced here: 91.3 us
  Pallas kernels  39 us (42%)
  other arithmetic  20.6 us (22%)
  local copies, waits for them, and re-layouts  13.2 us (14%)
  starting transfers between devices  11.6 us (13%)
  waiting for transfers between devices  5.06 us (5%)
  matrix products  1.67 us (2%)
    pallas_call x1, Pallas kernels, shards(): pl.pallas_call(tile_kernel, grid_spec=grid_spec, out_shape=jax.ShapeDtype...  39 us
    unnamed x7, other arithmetic  10.3 us
    concatenate x1, other arithmetic, with_halo(): block = jnp.concatenate([low, block, high], axis=dim)  8.15 us
    ppermute x2, starting transfers between devices, with_halo(): lax.ppermute(lax.slice_in_dim(block, block.shape[dim] - width, None, axis...  7.39 us
    ppermute x2, waiting for transfers between devices, with_halo(): lax.ppermute(lax.slice_in_dim(block, 0, width, axis=dim), axis, backward)  4.4 us
    ppermute x2, starting transfers between devices, with_halo(): lax.ppermute(lax.slice_in_dim(block, 0, width, axis=dim), axis, backward)  4.24 us
    another operation x2, local copies, waits for them, and re-layouts, shards(): windows.append(jnp.stack(shifted))  3.31 us
    convert_element_type x2, local copies, waits for them, and re-layouts, build_band(): return band.reshape(9, 4 * CIN, 2 * CMID).astype(jnp.bfloat16)  2.82 us
  transfers between devices with their start and end apart: 4, of which 2 were waited for; matrix products, arithmetic and copies ran while one was open for 9% of the time, Pallas kernels for 0%

profile of v1, /device:TPU:21, one launch (start us, length us, event | category | flops | bytes accessed | tf_op | source)
XLA Modules:
  0.0 91.3 jit_solution(16156706523821904394)
XLA Ops:
  0.0 1.0 %fusion.21 = (bf16[1,32,2048]{2,1,0:T(8,128)(2,1)S(1)}, bf16[1,32,2048]{2,1,0:T(8,128)(2,1)S(1)}) fusion(bf16[32,32,2048]{2,1,0:T(8,128)(2,1)} %param.7), kind=kLoop, calls=%fused_computation.66 | loop fusion | bytes 524288 | tf_op jit(solution)/shard_map/slice | solution.py:24
  1.0 3.1 %collective-permute-start = (bf16[1,32,2048]{2,1,0:T(8,128)(2,1)S(1)}, bf16[1,32,2048]{2,1,0:T(8,128)(2,1)S(1)}, u32[]{:S(2)}, u32[]{:S(2)}) collective-permute-start(bf16[1,32,2048]{2,1,0:T(8,128)(2,1)S(1)} %get-tuple-element.32), channel_id=1, source_target_pairs={{0,4},{4,8},{8,12},{12,16},{16,20},{20,24},{24,28},{1,5},{5,9},{9,... | collective-permute-start | bytes 393224 | tf_op jit(solution)/shard_map/ppermute | solution.py:21
  4.2 2.1 %collective-permute-start.1 = (bf16[1,32,2048]{2,1,0:T(8,128)(2,1)S(1)}, bf16[1,32,2048]{2,1,0:T(8,128)(2,1)S(1)}, u32[]{:S(2)}, u32[]{:S(2)}) collective-permute-start(bf16[1,32,2048]{2,1,0:T(8,128)(2,1)S(1)} %get-tuple-element.31), channel_id=1, source_target_pairs={{4,0},{8,4},{12,8},{16,12},{20,16},{24,20},{28,24},{5,1},{9,5},{13... | collective-permute-start | bytes 393224 | tf_op jit(solution)/shard_map/ppermute | solution.py:24
  6.3 1.7 %fusion.14 = bf16[3,3,4,64,2,128]{5,2,3,1,0,4:T(4,128)(2,1)S(1)} fusion(bf16[3,3,3,64,128]{4,3,2,1,0:T(8,128)(2,1)} %param.9, s32[4,2]{0,1:T(2,128)S(1)} %iota_subtract_fusion), kind=kOutput, calls=%fused_computation.25 | convolution fusion | flops 4128792 | bytes 1622048 | tf_op jit(solution)/shard_map/zod,xydcm->xyzcom/dot_general | solution.py:34
  8.2 0.7 reshape.112.flags_ref
  8.9 1.2 %copy.10 = bf16[3,3,4,64,2,128]{5,4,3,2,1,0:T(2,128)(2,1)S(1)} copy(bf16[3,3,4,64,2,128]{5,2,3,1,0,4:T(4,128)(2,1)S(1)} %fusion.14) | data formatting | bytes 2359296 | tf_op jit(solution)/shard_map/convert_element_type | solution.py:35
  10.1 1.6 %convert_element_type.16.band_ref = bf16[9,256,256]{2,1,0:T(8,128)(2,1)} reshape(bf16[3,3,4,64,2,128]{5,4,3,2,1,0:T(2,128)(2,1)S(1)} %copy.10) | data formatting | bytes 2359296 | tf_op jit(solution)/shard_map/convert_element_type | solution.py:35
  11.7 2.5 %constant_dynamic-update-slice_fusion.1 = bf16[34,32,2048]{2,1,0:T(8,128)(2,1)S(1)} fusion(bf16[34,32,2048]{2,1,0:T(8,128)(2,1)S(1)} %constant_dynamic-update-slice_fusion.2, bf16[32,32,2048]{2,1,0:T(8,128)(2,1)} %param.7), kind=kLoop, calls=%fused_computation.54 | loop fusion | bytes 8388608
  14.7 4.2 %collective-permute-start.2 = (bf16[34,1,2048]{2,1,0:T(2,128)(2,1)S(1)}, bf16[34,1,2048]{2,1,0:T(2,128)(2,1)S(1)}, u32[]{:S(2)}, u32[]{:S(2)}) collective-permute-start(bf16[34,1,2048]{2,1,0:T(2,128)(2,1)S(1)} %get-tuple-element.29), channel_id=1, source_target_pairs={{0,1},{1,2},{2,3},{4,5},{5,6},{6,7},{8,9},{9,10},{10,11},{12,13},{... | collective-permute-start | bytes 417800 | tf_op jit(solution)/shard_map/ppermute | solution.py:21
  19.0 2.1 %collective-permute-start.3 = (bf16[34,1,2048]{2,1,0:T(2,128)(2,1)S(1)}, bf16[34,1,2048]{2,1,0:T(2,128)(2,1)S(1)}, u32[]{:S(2)}, u32[]{:S(2)}) collective-permute-start(bf16[34,1,2048]{2,1,0:T(2,128)(2,1)S(1)} %get-tuple-element.30), channel_id=1, source_target_pairs={{1,0},{2,1},{3,2},{5,4},{6,5},{7,6},{9,8},{10,9},{11,10},{13,12},{... | collective-permute-start | bytes 417800 | tf_op jit(solution)/shard_map/ppermute | solution.py:24
  21.1 0.7 compare_convert_fusion.ind_ref
  22.4 4.4 %collective-permute-done.3 = bf16[34,1,2048]{2,1,0:T(2,128)(2,1)S(1)} collective-permute-done((bf16[34,1,2048]{2,1,0:T(2,128)(2,1)S(1)}, bf16[34,1,2048]{2,1,0:T(2,128)(2,1)S(1)}, u32[]{:S(2)}, u32[]{:S(2)}) %collective-permute-start.3) | collective-permute-done | bytes 139296 | tf_op jit(solution)/shard_map/ppermute | solution.py:24
  26.8 8.1 %fusion.5 = bf16[34,34,2176]{2,1,0:T(8,128)(2,1)S(1)} fusion(bf16[34,1,2048]{2,1,0:T(2,128)(2,1)S(1)} %collective-permute-done.3, bf16[34,32,2048]{2,1,0:T(8,128)(2,1)S(1)} %constant_dynamic-update-slice_fusion, bf16[34,1,2048]{2,1,0:T(2,128)(2,1)S(1)} %collective-permute-done.2), kind=kLoop, calls=%fused_computation.7 | loop fusion | flops 30185472 | bytes 9765888 | tf_op jit(solution)/shard_map/concatenate | solution.py:25
  35.6 2.7 %slice_bitcast_fusion.2 = (bf16[1,18,16,1152]{3,2,1,0:T(8,128)(2,1)S(1)}, bf16[1,18,16,1152]{3,2,1,0:T(8,128)(2,1)S(1)}, bf16[1,18,16,1152]{3,2,1,0:T(8,128)(2,1...) fusion(bf16[34,34,2176]{2,1,0:T(8,128)(2,1)S(1)} %fusion.5), kind=kLoop, calls=%fused_computation.28 | loop fusion | bytes 25214976 | tf_op jit(solution)/shard_map/stack | solution.py:127
  38.3 1.5 %fusion.6 = bf16[8,3,18,16,1152]{4,3,2,1,0:T(8,128)(2,1)} fusion(bf16[1,18,16,1152]{3,2,1,0:T(8,128)(2,1)S(1)} %get-tuple-element.26, bf16[1,18,16,1152]{3,2,1,0:T(8,128)(2,1)S(1)} %get-tuple-element.27, bf16[1,18,16,1152]{3,2,1,0:T(8,128)(2,1)S(1)} %get-tuple-element.28), kind=kLoop, calls=%fused_computation.9 | loop fusion | flops 5971967 | bytes 3981312
  39.8 1.4 %fusion.7 = bf16[8,3,18,16,1152]{4,3,2,1,0:T(8,128)(2,1)} fusion(bf16[8,3,18,16,1152]{4,3,2,1,0:T(8,128)(2,1)} %fusion.6, bf16[1,18,16,1152]{3,2,1,0:T(8,128)(2,1)S(1)} %get-tuple-element.22, bf16[1,18,16,1152]{3,2,1,0:T(8,128)(2,1)S(1)} %get-tuple-element.23, bf16[1,18,16,1152]{3,2,1,0:T(8,128)(2,1)S(1)} %get-tuple-element.25), kind=kLoop, calls=%fused_computation.11 | loop fusion | flops 5971968 | bytes 3981312
  41.2 1.5 %fusion.8 = bf16[8,3,18,16,1152]{4,3,2,1,0:T(8,128)(2,1)} fusion(bf16[8,3,18,16,1152]{4,3,2,1,0:T(8,128)(2,1)} %fusion.7, bf16[1,18,16,1152]{3,2,1,0:T(8,128)(2,1)S(1)} %get-tuple-element.19, bf16[1,18,16,1152]{3,2,1,0:T(8,128)(2,1)S(1)} %get-tuple-element.20, bf16[1,18,16,1152]{3,2,1,0:T(8,128)(2,1)S(1)} %get-tuple-element.21), kind=kLoop, calls=%fused_computation.13 | loop fusion | flops 5971968 | bytes 3981312
  42.6 1.4 %fusion.9 = bf16[8,3,18,16,1152]{4,3,2,1,0:T(8,128)(2,1)} fusion(bf16[8,3,18,16,1152]{4,3,2,1,0:T(8,128)(2,1)} %fusion.8, bf16[1,18,16,1152]{3,2,1,0:T(8,128)(2,1)S(1)} %get-tuple-element.16, bf16[1,18,16,1152]{3,2,1,0:T(8,128)(2,1)S(1)} %get-tuple-element.17, bf16[1,18,16,1152]{3,2,1,0:T(8,128)(2,1)S(1)} %get-tuple-element.18), kind=kLoop, calls=%fused_computation.15 | loop fusion | flops 5971968 | bytes 3981312
  44.1 1.5 %fusion.10 = bf16[8,3,18,16,1152]{4,3,2,1,0:T(8,128)(2,1)} fusion(bf16[8,3,18,16,1152]{4,3,2,1,0:T(8,128)(2,1)} %fusion.9, bf16[1,18,16,1152]{3,2,1,0:T(8,128)(2,1)S(1)} %get-tuple-element.13, bf16[1,18,16,1152]{3,2,1,0:T(8,128)(2,1)S(1)} %get-tuple-element.14, bf16[1,18,16,1152]{3,2,1,0:T(8,128)(2,1)S(1)} %get-tuple-element.15), kind=kLoop, calls=%fused_computation.17 | loop fusion | flops 5971968 | bytes 3981312
  45.6 1.4 %fusion.11 = bf16[8,3,18,16,1152]{4,3,2,1,0:T(8,128)(2,1)} fusion(bf16[8,3,18,16,1152]{4,3,2,1,0:T(8,128)(2,1)} %fusion.10, bf16[1,18,16,1152]{3,2,1,0:T(8,128)(2,1)S(1)} %get-tuple-element.10, bf16[1,18,16,1152]{3,2,1,0:T(8,128)(2,1)S(1)} %get-tuple-element.11, bf16[1,18,16,1152]{3,2,1,0:T(8,128)(2,1)S(1)} %get-tuple-element.12), kind=kLoop, calls=%fused_computation.19 | loop fusion | flops 5971968 | bytes 3981312
  47.0 1.5 %fusion.12 = bf16[8,3,18,16,1152]{4,3,2,1,0:T(8,128)(2,1)} fusion(bf16[8,3,18,16,1152]{4,3,2,1,0:T(8,128)(2,1)} %fusion.11, bf16[1,18,16,1152]{3,2,1,0:T(8,128)(2,1)S(1)} %get-tuple-element.7, bf16[1,18,16,1152]{3,2,1,0:T(8,128)(2,1)S(1)} %get-tuple-element.8, bf16[1,18,16,1152]{3,2,1,0:T(8,128)(2,1)S(1)} %get-tuple-element.9), kind=kLoop, calls=%fused_computation.21 | loop fusion | flops 5971968 | bytes 3981312
  48.6 1.4 %fusion.13.win_ref = bf16[8,3,18,16,1152]{4,3,2,1,0:T(8,128)(2,1)} fusion(bf16[8,3,18,16,1152]{4,3,2,1,0:T(8,128)(2,1)} %fusion.12, bf16[1,18,16,1152]{3,2,1,0:T(8,128)(2,1)S(1)} %get-tuple-element.24, bf16[1,18,16,1152]{3,2,1,0:T(8,128)(2,1)S(1)} %get-tuple-element.6, bf16[1,18,16,1152]{3,2,1,0:T(8,128)(2,1)S(1)} %get-tuple-element.5), kind=kLoop, calls=%fused_computation.23 | loop fusion | flops 5971968 | bytes 3981312 | tf_op jit(solution)/shard_map/stack | solution.py:128
  50.0 39.0 %shard_map.73 = bf16[8,64,1024]{2,1,0:T(8,128)(2,1)} custom-call(s32[8]{0:T(128)} %reshape.112.flags_ref, bf16[8,3,18,16,1152]{4,3,2,1,0:T(8,128)(2,1)} %fusion.13.win_ref, bf16[9,256,256]{2,1,0:T(8,128)(2,1)} %convert_element_type.16.band_ref, bf16[128,128]{1,0:T(8,128)(2,1)} %compare_convert_fusion.ind_ref, f32[1,128]{1,0:T(1,128)} %bitcast.100, ...), custom_call_target="tpu_custom_call" | custom-call | tf_op jit(solution)/shard_map/pallas_call | solution.py:153
  89.0 2.3 %copy.11 = bf16[2,8,2,8,2,1024]{5,3,4,2,1,0:T(8,128)(2,1)} copy(bf16[2,8,2,8,2,1024]{5,3,1,4,2,0:T(8,128)(2,1)} %bitcast.98) | data formatting | bytes 2097152 | tf_op jit(solution)/shard_map/transpose | solution.py:168
  (13 shorter events, 1.9 us)
Async XLA Ops:
  0.0 8.0 %copy-start = (s32[16,2,2]{0,2,1:T(2,128)S(1)}, s32[16,2,2]{0,2,1:T(2,128)}, u32[]{:S(2)}) copy-start(s32[16,2,2]{0,2,1:T(2,128)} %param.8) | copy-start | bytes 772
  1.0 10.7 %collective-permute-start = (bf16[1,32,2048]{2,1,0:T(8,128)(2,1)S(1)}, bf16[1,32,2048]{2,1,0:T(8,128)(2,1)S(1)}, u32[]{:S(2)}, u32[]{:S(2)}) collective-permute-start(bf16[1,32,2048]{2,1,0:T(8,128)(2,1)S(1)} %get-tuple-element.32), channel_id=1, source_target_pairs={{0,4},{4,8},{8,12},{12,16},{16,20},{20,24},{24,28},{1,5},{5,9},{9,... | collective-permute-start | bytes 393224 | tf_op jit(solution)/shard_map/ppermute | solution.py:21
  4.2 10.0 %collective-permute-start.1 = (bf16[1,32,2048]{2,1,0:T(8,128)(2,1)S(1)}, bf16[1,32,2048]{2,1,0:T(8,128)(2,1)S(1)}, u32[]{:S(2)}, u32[]{:S(2)}) collective-permute-start(bf16[1,32,2048]{2,1,0:T(8,128)(2,1)S(1)} %get-tuple-element.31), channel_id=1, source_target_pairs={{4,0},{8,4},{12,8},{16,12},{20,16},{24,20},{28,24},{5,1},{9,5},{13... | collective-permute-start | bytes 393224 | tf_op jit(solution)/shard_map/ppermute | solution.py:24
  14.7 7.7 %collective-permute-start.2 = (bf16[34,1,2048]{2,1,0:T(2,128)(2,1)S(1)}, bf16[34,1,2048]{2,1,0:T(2,128)(2,1)S(1)}, u32[]{:S(2)}, u32[]{:S(2)}) collective-permute-start(bf16[34,1,2048]{2,1,0:T(2,128)(2,1)S(1)} %get-tuple-element.29), channel_id=1, source_target_pairs={{0,1},{1,2},{2,3},{4,5},{5,6},{6,7},{8,9},{9,10},{10,11},{12,13},{... | collective-permute-start | bytes 417800 | tf_op jit(solution)/shard_map/ppermute | solution.py:21
  19.0 7.9 %collective-permute-start.3 = (bf16[34,1,2048]{2,1,0:T(2,128)(2,1)S(1)}, bf16[34,1,2048]{2,1,0:T(2,128)(2,1)S(1)}, u32[]{:S(2)}, u32[]{:S(2)}) collective-permute-start(bf16[34,1,2048]{2,1,0:T(2,128)(2,1)S(1)} %get-tuple-element.30), channel_id=1, source_target_pairs={{1,0},{2,1},{3,2},{5,4},{6,5},{7,6},{9,8},{10,9},{11,10},{13,12},{... | collective-permute-start | bytes 417800 | tf_op jit(solution)/shard_map/ppermute | solution.py:24
